TPU v7x, 256 devices: a whole 4x4x8 slice. The times are simulated.
256 devices in a mesh: layer: 32 (over z, x), row: 2 (over core), col: 4 (over y).
Axes of the slice: x: 4, y: 4, z: 8, core: 2. Of those that a mesh axis runs over, the one named last changes fastest.
Arguments:
- left_factor: float32 [2048, 65536], P('row', ('layer', 'col')), may hold values from -6 to 6
- right_factor: float32 [65536, 4096], P(('layer', 'row'), 'col'), may hold values from -0.15625 to 0.15625
- left_pattern: int32 [32, 1024], P('row', ('layer', 'col')), may hold values 0 or 1
- right_pattern: int32 [1024, 64], P(('layer', 'row'), 'col'), may hold values 0 or 1
- product_pattern: int32 [32, 64], P('row', 'col'), may hold values 0 or 1
Outputs:
- product: float32 [2048, 4096], P(('layer', 'row'), 'col')
All inputs are finite; a program needn't handle non-finite values. No bound on the sum of `left_pattern` or of `right_pattern` or of `product_pattern` on one device may be relied on, other than what follows from the above.
Results may differ from a plain program's by a relative error of at most 0.000092.
Values sent between devices are 32-bit elements; how exact they have to be, the bound alone decides.
No kernel may reach another device: no remote copies, remote signals or barrier semaphores. Data moves between devices by JAX's collectives and lax.ppermute only.
A program may use at most 128 MiB of HBM per device.

v0:
```python
import jax
import jax.numpy as jnp
from jax import lax
from jax.sharding import Mesh
from jax.sharding import PartitionSpec as P

BS = 64


def expand(pattern):
    return jnp.repeat(jnp.repeat(pattern.astype(jnp.float32), BS, axis=0), BS, axis=1)


def body(left_factor, right_factor, left_pattern, right_pattern, product_pattern):
    left = left_factor * expand(left_pattern)
    right = right_factor * expand(right_pattern)
    left_whole = lax.all_gather(left, "col", axis=1, tiled=True)
    partial_sum = jnp.dot(
        left_whole,
        lax.all_gather(right, "row", axis=0, tiled=True),
        preferred_element_type=jnp.float32,
        precision=lax.Precision.HIGHEST,
    )
    kept = partial_sum * expand(product_pattern)
    kept = lax.psum_scatter(kept, "lz", scatter_dimension=0, tiled=True)
    return lax.psum_scatter(kept, "lx", scatter_dimension=0, tiled=True)


def solution(mesh):
    n_layer, n_row, n_col = mesh.devices.shape
    n_x = 4 if n_layer % 4 == 0 else 1
    split = Mesh(
        mesh.devices.reshape(n_layer // n_x, n_x, n_row, n_col), ("lz", "lx", "row", "col")
    )
    layer = ("lz", "lx")
    return jax.shard_map(
        body,
        mesh=split,
        in_specs=(
            P("row", (*layer, "col")),
            P((*layer, "row"), "col"),
            P("row", (*layer, "col")),
            P((*layer, "row"), "col"),
            P("row", "col"),
        ),
        out_specs=P((*layer, "row"), "col"),
        check_vma=False,
    )
```

profile of v0, /device:TPU:8, one launch (start us, length us, event | category | flops | bytes accessed | tf_op | source)
XLA Modules:
  0.0 280.0 jit_solution(4011034189807476211)
XLA Ops:
  6.5 0.0 copy-start
  6.5 0.0 all-gather.5.cloned.1.call-start
  6.5 5.4 %copy.9 = f32[1024,1024]{0,1:T(8,128)} copy(f32[1024,1024]{1,0:T(8,128)} %param.6) | data formatting | bytes 8388608 | tf_op args[1]
  11.9 0.0 copy-done
  11.9 0.1 copy.8
  12.0 0.1 broadcast_in_dim.20
  12.1 0.1 reshape.20
  12.2 5.0 %bitcast_multiply_fusion = f32[1024,1024]{0,1:T(8,128)} fusion(f32[1024,1024]{0,1:T(8,128)} %copy.9, f32[1024,16]{0,1:T(8,128)S(1)} %reshape.20), kind=kLoop, calls=%fused_computation | loop fusion | flops 1048576 | bytes 8454144 | tf_op jit(solution)/shard_map/mul | solution.py:16
  17.2 0.0 all-gather.5.cloned.1.call-update
  17.2 0.0 all-gather.3.cloned.1.call-start
  17.3 1.9 copy.7
  19.2 0.0 copy-done.2
  19.2 0.0 copy-start.1
  19.3 0.1 broadcast_in_dim.18
  19.3 0.1 reshape.18
  19.4 1.5 bitcast_multiply_fusion.1
  21.0 0.0 all-gather.3.cloned.1.call-update
  21.0 0.0 reduce-scatter.3.cloned.1.call-start
  21.0 0.0 copy-done.1
  21.0 0.1 copy.10
  21.1 0.1 broadcast_in_dim.22
  21.2 0.1 reshape.22
  21.3 2.5 broadcast_in_dim.23
  23.8 5.4 %copy.11 = f32[1024,1024]{1,0:T(8,128)} copy(f32[1024,1024]{0,1:T(8,128)} %bitcast.13) | data formatting | bytes 8388608 | tf_op jit(solution)/shard_map/reshape | solution.py:11
  29.2 16.3 %all-gather.5.cloned.1.call-done = f32[2048,1024]{0,1:T(8,128)} async-done(((f32[1024,1024]{0,1:T(8,128)}), f32[2048,1024]{0,1:T(8,128)}) %all-gather.5.cloned.1.call-update) | async-done | bytes 8388624 | tf_op jit(solution)/shard_map/all_gather | solution.py:20
  45.5 88.7 %all-gather.3.cloned.1.call-done = f32[1024,2048]{0,1:T(8,128)} async-done(((f32[1024,512]{0,1:T(8,128)}), f32[1024,2048]{0,1:T(8,128)}) %all-gather.3.cloned.1.call-update) | async-done | bytes 8388624 | tf_op jit(solution)/shard_map/all_gather | solution.py:17
  134.2 57.5 %convolution_multiply_fusion = f32[1024,1024]{1,0:T(8,128)} fusion(f32[1024,1024]{1,0:T(8,128)} %copy.11, f32[1024,2048]{0,1:T(8,128)} %all-gather.3.cloned.1.call-done, f32[2048,1024]{0,1:T(8,128)} %all-gather.5.cloned.1.call-done), kind=kOutput, calls=%fused_computation.1 | convolution fusion | flops 25770852352 | bytes 25165824 | tf_op jit(solution)/shard_map/dot_general | solution.py:18
  191.7 0.0 reduce-scatter.3.cloned.1.call-update
  191.7 0.0 reduce-scatter.5.cloned.1.call-start
  191.8 56.4 %reduce-scatter.3.cloned.1.call-done = f32[128,1024]{1,0:T(8,128)} async-done(((f32[1024,1024]{1,0:T(8,128)}), f32[128,1024]{1,0:T(8,128)}) %reduce-scatter.3.cloned.1.call-update) | async-done | bytes 524304 | tf_op jit(solution)/shard_map/reduce_scatter | solution.py:25
  248.2 0.0 reduce-scatter.5.cloned.1.call-update
  248.2 25.2 %reduce-scatter.5.cloned.1.call-done = f32[32,1024]{1,0:T(8,128)} async-done(((f32[128,1024]{1,0:T(8,128)}), f32[32,1024]{1,0:T(8,128)}) %reduce-scatter.5.cloned.1.call-update) | async-done | bytes 131088 | tf_op jit(solution)/shard_map/reduce_scatter | solution.py:26
  (4 shorter events, 0.0 us)
Async XLA Ops:
  6.5 5.4 %copy-start = (s32[16,16]{1,0:T(8,128)S(1)}, s32[16,16]{1,0:T(8,128)}, u32[]{:S(2)}) copy-start(s32[16,16]{1,0:T(8,128)} %param.8) | copy-start | bytes 3076
  6.5 38.9 %all-gather.5.cloned.1.call-start = ((), (), s32[]{:S(2)}) async-start(), calls=%async_computation.3 | async-start | bytes 12582912 | tf_op jit(solution)/shard_map/all_gather | solution.py:20
  17.2 2.0 copy-start.2
  17.2 117.0 %all-gather.3.cloned.1.call-start = ((), (), s32[]{:S(2)}) async-start(), calls=%async_computation.2 | async-start | bytes 10485760 | tf_op jit(solution)/shard_map/all_gather | solution.py:17
  19.2 1.8 copy-start.1
  21.0 227.2 %reduce-scatter.3.cloned.1.call-start = ((), (), s32[]{:S(2)}) async-start(), calls=%async_computation.4 | async-start | bytes 4718592 | tf_op jit(solution)/shard_map/reduce_scatter | solution.py:25
  191.7 81.7 %reduce-scatter.5.cloned.1.call-start = ((), (), s32[]{:S(2)}) async-start(), calls=%async_computation.5 | async-start | bytes 655360 | tf_op jit(solution)/shard_map/reduce_scatter | solution.py:26
Sparse Core Ops, SparseCore 0:
  17.4 28.0 all-gather.4
  47.3 86.8 all-gather.2
  191.8 56.3 reduce-scatter.2
  250.6 22.7 reduce-scatter.4
where the time goes:
time: 280 us
  waiting for transfers between devices  187 us (67%)
  matrix products  57.5 us (21%)
  local copies, waits for them, and re-layouts  15.9 us (6%)
  between operations  13.2 us (5%)
  other arithmetic  6.55 us (2%)
    all_gather x1, waiting for transfers between devices, body(): left_whole = lax.all_gather(left, 'col', axis=1, tiled=True)  88.7 us
    dot_general x1, matrix products, body(): jnp.dot(left_whole, lax.all_gather(right, 'row', axis=0, tiled=True), pre...  57.5 us
    reduce_scatter x1, waiting for transfers between devices, body(): kept = lax.psum_scatter(kept, 'lz', scatter_dimension=0, tiled=True)  56.4 us
    reduce_scatter x1, waiting for transfers between devices, body(): return lax.psum_scatter(kept, 'lx', scatter_dimension=0, tiled=True)  25.2 us
    all_gather x1, waiting for transfers between devices, body(): lax.all_gather(right, 'row', axis=0, tiled=True)  16.3 us
    unnamed x8, local copies, waits for them, and re-layouts  7.33 us
  transfers between devices with their start and end apart: 4, of which 4 were waited for; matrix products, arithmetic and copies ran while one was open for 4% of the time, Pallas kernels for 0%

commit v1 on v0

--- a/solution.py
+++ b/solution.py
@@ -17,7 +17,9 @@
     left_whole = lax.all_gather(left, "col", axis=1, tiled=True)
     partial_sum = jnp.dot(
         left_whole,
-        lax.all_gather(right, "row", axis=0, tiled=True),
+        jnp.concatenate(
+            lax.all_to_all(jnp.stack([right] * lax.axis_size("row")), "row", 0, 0), axis=0
+        ),
         preferred_element_type=jnp.float32,
         precision=lax.Precision.HIGHEST,
     )

time: 280 us -> 220 us (0.79)
  waiting for transfers between devices: 187 us -> 133 us
  matrix products: 57.5 us -> 31.9 us
  local copies, waits for them, and re-layouts: 15.9 us -> 24.6 us
  starting transfers between devices: 0.13 us -> 7.75 us
    all_gather x1, waiting for transfers between devices: 88.7 us -> 51.4 us  [body(): left_whole = lax.all_gather(left, 'col', axis=1, tiled=True)]
    dot_general x1, matrix products: 57.5 us -> 31.9 us  [body(): jnp.dot(left_whole, jnp.concatenate(lax.all_to_all(jnp.stack([right] * la...]
    all_gather x1 -> x0, waiting for transfers between devices: 16.3 us -> none  [body(): lax.all_gather(right, 'row', axis=0, tiled=True)]
    all_to_all x0 -> x1, local copies, waits for them, and re-layouts: none -> 8.75 us  [body(): lax.all_to_all(jnp.stack([right] * lax.axis_size('row')), 'row', 0, 0)]
    all_to_all x0 -> x1, starting transfers between devices: none -> 7.67 us  [body(): lax.all_to_all(jnp.stack([right] * lax.axis_size('row')), 'row', 0, 0)]
    another operation x0 -> x1, other arithmetic: none -> 4.29 us  [body(): jnp.stack([right] * lax.axis_size('row'))]
  transfers between devices with their start and end apart: 4 -> 4, of which waited for: 4 -> 3; matrix products, arithmetic and copies ran while one was open for 4% -> 13% of each run, Pallas kernels for 0% -> 0%
where the time goes in v1:
time: 220 us; the launch traced here: 219 us
  waiting for transfers between devices  133 us (60%)
  matrix products  31.9 us (14%)
  local copies, waits for them, and re-layouts  24.6 us (11%)
  between operations  13.2 us (6%)
  other arithmetic  8.5 us (4%)
  starting transfers between devices  7.75 us (4%)
    reduce_scatter x1, waiting for transfers between devices, body(): kept = lax.psum_scatter(kept, 'lz', scatter_dimension=0, tiled=True)  56.4 us
    all_gather x1, waiting for transfers between devices, body(): left_whole = lax.all_gather(left, 'col', axis=1, tiled=True)  51.4 us
    dot_general x1, matrix products, body(): jnp.dot(left_whole, jnp.concatenate(lax.all_to_all(jnp.stack([right] * la...  31.9 us
    reduce_scatter x1, waiting for transfers between devices, body(): return lax.psum_scatter(kept, 'lx', scatter_dimension=0, tiled=True)  25.3 us
    all_to_all x1, local copies, waits for them, and re-layouts, body(): lax.all_to_all(jnp.stack([right] * lax.axis_size('row')), 'row', 0, 0)  8.75 us
    all_to_all x1, starting transfers between devices, body(): lax.all_to_all(jnp.stack([right] * lax.axis_size('row')), 'row', 0, 0)  7.67 us
    unnamed x8, local copies, waits for them, and re-layouts  7.32 us
    reshape x1, local copies, waits for them, and re-layouts, expand(): jnp.repeat(jnp.repeat(pattern.astype(jnp.float32), BS, axis=0), BS, axis=1)  5.4 us
  transfers between devices with their start and end apart: 4, of which 3 were waited for; matrix products, arithmetic and copies ran while one was open for 13% of the time, Pallas kernels for 0%

profile of v1, /device:TPU:8, one launch (start us, length us, event | category | flops | bytes accessed | tf_op | source)
XLA Modules:
  0.0 219.2 jit_solution(13788924196487662262)
XLA Ops:
  6.5 0.0 all-gather.2.cloned.1.call-start
  6.5 1.9 copy.12
  8.5 0.0 copy-done.2
  8.5 0.1 broadcast_in_dim.18
  8.6 0.1 reshape.21
  8.7 1.5 bitcast_multiply_fusion.1
  10.2 0.0 all-gather.2.cloned.1.call-update
  10.2 0.0 copy-start
  10.2 5.4 %copy.14 = f32[1024,1024]{0,1:T(8,128)} copy(f32[1024,1024]{1,0:T(8,128)} %param.6) | data formatting | bytes 8388608 | tf_op args[1]
  15.6 0.0 copy-done
  15.6 0.1 copy.13
  15.7 0.1 broadcast_in_dim.20
  15.8 0.1 reshape.23
  15.9 2.7 %bitcast_multiply_fusion = f32[1024,1024]{0,1:T(8,128)S(1)} fusion(f32[1024,1024]{0,1:T(8,128)} %copy.14, f32[1024,16]{0,1:T(8,128)S(1)} %reshape.23), kind=kLoop, calls=%fused_computation.1 | loop fusion | flops 1048576 | bytes 8454144 | tf_op jit(solution)/shard_map/mul | solution.py:16
  18.6 4.3 %pad_maximum_fusion = f32[2,1024,1024]{1,2,0:T(8,128)} fusion(f32[1,1024,1024]{1,2,0:T(8,128)S(1)} %bitcast.15), kind=kLoop, calls=%fused_computation | loop fusion | flops 2097152 | bytes 12582912 | tf_op jit(solution)/shard_map/stack | solution.py:21
  22.9 7.7 %all-to-all-start = ((f32[2,1024,1024]{1,2,0:T(8,128)}), f32[2,1024,1024]{1,2,0:T(8,128)}, u32[]{:S(2)}, u32[]{:S(2)}) async-start(f32[2,1024,1024]{1,2,0:T(8,128)} %pad_maximum_fusion), calls=%async_computation | async-start | bytes 16777216 | tf_op jit(solution)/shard_map/all_to_all | solution.py:21
  30.5 0.0 reduce-scatter.3.cloned.1.call-start
  30.6 0.0 copy-done.1
  30.6 0.1 copy.16
  30.7 0.1 broadcast_in_dim.22
  30.8 0.1 reshape.26
  30.9 2.5 %broadcast_in_dim.23 = f32[1024,16,64]{0,2,1:T(8,128)} broadcast(f32[1024,16]{0,1:T(8,128)S(1)} %reshape.26), dimensions={0,1} | broadcast | bytes 4259840 | tf_op jit(solution)/shard_map/broadcast_in_dim | solution.py:11
  33.3 5.4 %copy.17 = f32[1024,1024]{1,0:T(8,128)} copy(f32[1024,1024]{0,1:T(8,128)} %bitcast.16) | data formatting | bytes 8388608 | tf_op jit(solution)/shard_map/reshape | solution.py:11
  38.7 0.0 all-to-all-done
  38.7 8.7 %copy.15 = f32[2,1024,1024]{2,1,0:T(8,128)} copy(f32[2,1024,1024]{1,2,0:T(8,128)} %all-to-all-done) | data formatting | bytes 16777216 | tf_op jit(solution)/shard_map/all_to_all | solution.py:21
  47.5 51.4 %all-gather.2.cloned.1.call-done = f32[1024,2048]{0,1:T(8,128)} async-done(((f32[1024,512]{0,1:T(8,128)}), f32[1024,2048]{0,1:T(8,128)}) %all-gather.2.cloned.1.call-update) | async-done | bytes 8388624 | tf_op jit(solution)/shard_map/all_gather | solution.py:17
  98.9 31.9 %convolution_multiply_fusion = f32[1024,1024]{1,0:T(8,128)} fusion(f32[1024,1024]{1,0:T(8,128)} %copy.17, f32[1024,2048]{0,1:T(8,128)} %all-gather.2.cloned.1.call-done, f32[2048,1024]{1,0:T(8,128)} %bitcast.17), kind=kOutput, calls=%fused_computation.2 | convolution fusion | flops 25770852352 | bytes 25165824 | tf_op jit(solution)/shard_map/dot_general | solution.py:18
  130.8 0.0 reduce-scatter.3.cloned.1.call-update
  130.8 0.0 reduce-scatter.5.cloned.1.call-start
  130.9 56.4 %reduce-scatter.3.cloned.1.call-done = f32[128,1024]{1,0:T(8,128)} async-done(((f32[1024,1024]{1,0:T(8,128)}), f32[128,1024]{1,0:T(8,128)}) %reduce-scatter.3.cloned.1.call-update) | async-done | bytes 524304 | tf_op jit(solution)/shard_map/reduce_scatter | solution.py:27
  187.3 0.0 reduce-scatter.5.cloned.1.call-update
  187.3 25.3 %reduce-scatter.5.cloned.1.call-done = f32[32,1024]{1,0:T(8,128)} async-done(((f32[128,1024]{1,0:T(8,128)}), f32[32,1024]{1,0:T(8,128)}) %reduce-scatter.5.cloned.1.call-update) | async-done | bytes 131088 | tf_op jit(solution)/shard_map/reduce_scatter | solution.py:28
  (5 shorter events, 0.0 us)
Async XLA Ops:
  6.5 1.9 copy-start.2
  6.5 92.3 %all-gather.2.cloned.1.call-start = ((), (), s32[]{:S(2)}) async-start(), calls=%async_computation.3 | async-start | bytes 10485760 | tf_op jit(solution)/shard_map/all_gather | solution.py:17
  10.2 5.4 %copy-start = (s32[16,16]{1,0:T(8,128)S(1)}, s32[16,16]{1,0:T(8,128)}, u32[]{:S(2)}) copy-start(s32[16,16]{1,0:T(8,128)} %param.8) | copy-start | bytes 3076
  22.9 7.7 %copy-start.1 = (s32[16,16]{1,0:T(8,128)S(1)}, s32[16,16]{1,0:T(8,128)}, u32[]{:S(2)}) copy-start(s32[16,16]{1,0:T(8,128)} %param.9) | copy-start | bytes 3076
  22.9 15.9 %all-to-all-start = ((f32[2,1024,1024]{1,2,0:T(8,128)}), f32[2,1024,1024]{1,2,0:T(8,128)}, u32[]{:S(2)}, u32[]{:S(2)}) async-start(f32[2,1024,1024]{1,2,0:T(8,128)} %pad_maximum_fusion), calls=%async_computation | async-start | bytes 16777216 | tf_op jit(solution)/shard_map/all_to_all | solution.py:21
  30.5 156.8 %reduce-scatter.3.cloned.1.call-start = ((), (), s32[]{:S(2)}) async-start(), calls=%async_computation.4 | async-start | bytes 4718592 | tf_op jit(solution)/shard_map/reduce_scatter | solution.py:27
  130.8 81.8 %reduce-scatter.5.cloned.1.call-start = ((), (), s32[]{:S(2)}) async-start(), calls=%async_computation.5 | async-start | bytes 655360 | tf_op jit(solution)/shard_map/reduce_scatter | solution.py:28
Sparse Core Ops, SparseCore 0:
  10.3 88.4 all-gather.1
  131.0 56.3 reduce-scatter.2
  189.9 22.7 reduce-scatter.4

commit v2 on v0

--- a/solution.py
+++ b/solution.py
@@ -7,6 +7,22 @@
 BS = 64
 
 
+def collect(x, axis, dim):
+    ways, here, lap = (lax.axis_size(axis), lax.axis_index(axis), x.shape[dim])
+    shape = [n * ways if d == dim else n for d, n in enumerate(x.shape)]
+    full = lax.dynamic_update_slice_in_dim(jnp.zeros(shape, x.dtype), x, here * lap, axis=dim)
+    going_up = going_down = x
+    for far in range(1, ways // 2 + 1):
+        going_up = lax.ppermute(going_up, axis, [(d, (d + 1) % ways) for d in range(ways)])
+        full = lax.dynamic_update_slice_in_dim(full, going_up, (here - far) % ways * lap, axis=dim)
+        if 2 * far < ways:
+            going_down = lax.ppermute(going_down, axis, [(d, (d - 1) % ways) for d in range(ways)])
+            full = lax.dynamic_update_slice_in_dim(
+                full, going_down, (here + far) % ways * lap, axis=dim
+            )
+    return full
+
+
 def expand(pattern):
     return jnp.repeat(jnp.repeat(pattern.astype(jnp.float32), BS, axis=0), BS, axis=1)
 
@@ -14,7 +30,7 @@
 def body(left_factor, right_factor, left_pattern, right_pattern, product_pattern):
     left = left_factor * expand(left_pattern)
     right = right_factor * expand(right_pattern)
-    left_whole = lax.all_gather(left, "col", axis=1, tiled=True)
+    left_whole = collect(left, "col", 1)
     partial_sum = jnp.dot(
         left_whole,
         lax.all_gather(right, "row", axis=0, tiled=True),

time: 280 us -> 271 us (0.968)
  waiting for transfers between devices: 187 us -> 162 us
  local copies, waits for them, and re-layouts: 15.9 us -> 28 us
  starting transfers between devices: 0.13 us -> 3.82 us
    all_gather x1 -> x0, waiting for transfers between devices: 88.7 us -> none  [body(): left_whole = lax.all_gather(left, 'col', axis=1, tiled=True)]
    ppermute x0 -> x3, waiting for transfers between devices: none -> 77.6 us  [the longest x2 77.6 us: collect(): lax.ppermute(going_up, axis, [(d, (d + 1) % ways) for d in range(ways)])]
    all_gather x1, waiting for transfers between devices: 16.3 us -> 0.01 us  [body(): lax.all_gather(right, 'row', axis=0, tiled=True)]
    dynamic_update_slice x0 -> x3, local copies, waits for them, and re-layouts: none -> 7.81 us  [the longest x2 4.64 us: collect(): lax.dynamic_update_slice_in_dim(full, going_up, (here - far) % ways * lap...]
    ppermute x0 -> x3, starting transfers between devices: none -> 3.74 us  [the longest x2 3.15 us: collect(): lax.ppermute(going_up, axis, [(d, (d + 1) % ways) for d in range(ways)])]
    unnamed x8 -> x10, local copies, waits for them, and re-layouts: 7.33 us -> 10.6 us
  transfers between devices with their start and end apart: 4 -> 6, of which waited for: 4 -> 4; matrix products, arithmetic and copies ran while one was open for 4% -> 8% of each run, Pallas kernels for 0% -> 0%
where the time goes in v2:
time: 271 us
  waiting for transfers between devices  162 us (60%)
  matrix products  57.5 us (21%)
  local copies, waits for them, and re-layouts  28 us (10%)
  between operations  13.2 us (5%)
  other arithmetic  6.85 us (3%)
  starting transfers between devices  3.82 us (1%)
    ppermute x2, waiting for transfers between devices, collect(): lax.ppermute(going_up, axis, [(d, (d + 1) % ways) for d in range(ways)])  77.6 us
    reduce_scatter x1, waiting for transfers between devices, body(): kept = lax.psum_scatter(kept, 'lz', scatter_dimension=0, tiled=True)  58.5 us
    dot_general x1, matrix products, body(): jnp.dot(left_whole, lax.all_gather(right, 'row', axis=0, tiled=True), pre...  57.5 us
    reduce_scatter x1, waiting for transfers between devices, body(): return lax.psum_scatter(kept, 'lx', scatter_dimension=0, tiled=True)  25.3 us
    unnamed x10, local copies, waits for them, and re-layouts  10.6 us
  transfers between devices with their start and end apart: 6, of which 4 were waited for; matrix products, arithmetic and copies ran while one was open for 8% of the time, Pallas kernels for 0%

profile of v2, /device:TPU:8, one launch (start us, length us, event | category | flops | bytes accessed | tf_op | source)
XLA Modules:
  0.0 270.8 jit_solution(4007710700812664650)
XLA Ops:
  6.5 5.4 %copy.9 = f32[1024,1024]{0,1:T(8,128)} copy(f32[1024,1024]{1,0:T(8,128)} %param.6) | data formatting | bytes 8388608 | tf_op args[1]
  11.9 0.1 copy.8
  12.0 0.1 broadcast_in_dim.24
  12.1 0.1 reshape.20
  12.2 5.0 %bitcast_multiply_fusion = f32[1024,1024]{0,1:T(8,128)} fusion(f32[1024,1024]{0,1:T(8,128)} %copy.9, f32[1024,16]{0,1:T(8,128)S(1)} %reshape.20), kind=kLoop, calls=%fused_computation | loop fusion | flops 1048576 | bytes 8454144 | tf_op jit(solution)/shard_map/mul | solution.py:32
  17.2 0.0 all-gather.2.cloned.1.call-update
  17.2 0.0 reduce-scatter.3.cloned.1.call-start
  17.3 1.9 copy.7
  19.2 0.1 broadcast_in_dim.22
  19.3 0.1 reshape.18
  19.4 1.1 broadcast_in_dim.21
  20.5 1.8 constant_dynamic-update-slice_fusion.3
  22.3 3.2 %copy-done = f32[1024,2048]{0,1:T(8,128)} copy-done((f32[1024,2048]{0,1:T(8,128)}, f32[1024,2048]{0,1:T(8,128)S(1)}, u32[]{:S(2)}) %copy-start) | copy-done | bytes 8388632
  25.5 1.6 collective-permute-start
  27.1 0.6 collective-permute-start.1
  27.7 45.4 %collective-permute-done = f32[1024,512]{0,1:T(8,128)S(1)} collective-permute-done((f32[1024,512]{0,1:T(8,128)}, f32[1024,512]{0,1:T(8,128)S(1)}, u32[]{:S(2)}, u32[]{:S(2)}) %collective-permute-start) | collective-permute-done | bytes 2097184 | tf_op jit(solution)/shard_map/ppermute | solution.py:16
  73.1 1.6 collective-permute-start.2
  74.7 0.1 copy.10
  74.8 0.1 broadcast_in_dim.26
  74.9 0.1 reshape.22
  75.0 2.5 broadcast_in_dim.27
  77.5 5.4 %copy.11 = f32[1024,1024]{1,0:T(8,128)} copy(f32[1024,1024]{0,1:T(8,128)} %bitcast.13) | data formatting | bytes 8388608 | tf_op jit(solution)/shard_map/reshape | solution.py:27
  82.9 1.5 constant_dynamic-update-slice_fusion.2
  84.4 3.2 %constant_dynamic-update-slice_fusion.1 = f32[1024,2048]{0,1:T(8,128)} fusion(f32[1024,2048]{0,1:T(8,128)} %constant_dynamic-update-slice_fusion.2, f32[1024,512]{0,1:T(8,128)} %collective-permute-done.1, s32[]{:T(128)S(6)} %select_n.31), kind=kLoop, calls=%fused_computation.4 | loop fusion | bytes 4194308 | tf_op jit(solution)/shard_map/dynamic_update_slice | solution.py:20
  87.5 32.2 %collective-permute-done.2 = f32[1024,512]{0,1:T(8,128)} collective-permute-done((f32[1024,512]{0,1:T(8,128)S(1)}, f32[1024,512]{0,1:T(8,128)}, u32[]{:S(2)}, u32[]{:S(2)}) %collective-permute-start.2) | collective-permute-done | bytes 2097184 | tf_op jit(solution)/shard_map/ppermute | solution.py:16
  119.7 3.1 %constant_dynamic-update-slice_fusion = f32[1024,2048]{0,1:T(8,128)} fusion(f32[1024,2048]{0,1:T(8,128)} %constant_dynamic-update-slice_fusion.1, f32[1024,512]{0,1:T(8,128)} %collective-permute-done.2, s32[]{:T(128)S(6)} %select_n.33), kind=kLoop, calls=%fused_computation.3 | loop fusion | bytes 4194308 | tf_op jit(solution)/shard_map/dynamic_update_slice | solution.py:17
  122.9 57.5 %convolution_multiply_fusion = f32[1024,1024]{1,0:T(8,128)} fusion(f32[1024,1024]{1,0:T(8,128)} %copy.11, f32[1024,2048]{0,1:T(8,128)} %constant_dynamic-update-slice_fusion, f32[2048,1024]{0,1:T(8,128)} %all-gather.2.cloned.1.call-done), kind=kOutput, calls=%fused_computation.1 | convolution fusion | flops 25770852352 | bytes 25165824 | tf_op jit(solution)/shard_map/dot_general | solution.py:34
  180.4 0.0 reduce-scatter.3.cloned.1.call-update
  180.4 0.0 reduce-scatter.5.cloned.1.call-start
  180.4 58.5 %reduce-scatter.3.cloned.1.call-done = f32[128,1024]{1,0:T(8,128)} async-done(((f32[1024,1024]{1,0:T(8,128)}), f32[128,1024]{1,0:T(8,128)}) %reduce-scatter.3.cloned.1.call-update) | async-done | bytes 524304 | tf_op jit(solution)/shard_map/reduce_scatter | solution.py:41
  238.9 0.0 reduce-scatter.5.cloned.1.call-update
  239.0 25.3 %reduce-scatter.5.cloned.1.call-done = f32[32,1024]{1,0:T(8,128)} async-done(((f32[128,1024]{1,0:T(8,128)}), f32[32,1024]{1,0:T(8,128)}) %reduce-scatter.5.cloned.1.call-update) | async-done | bytes 131088 | tf_op jit(solution)/shard_map/reduce_scatter | solution.py:42
  (13 shorter events, 0.0 us)
Async XLA Ops:
  6.5 5.4 %copy-start.1 = (s32[16,16]{1,0:T(8,128)S(1)}, s32[16,16]{1,0:T(8,128)}, u32[]{:S(2)}) copy-start(s32[16,16]{1,0:T(8,128)} %param.8) | copy-start | bytes 3076
  6.5 116.3 %all-gather.2.cloned.1.call-start = ((), (), s32[]{:S(2)}) async-start(), calls=%async_computation.2 | async-start | bytes 12582912 | tf_op jit(solution)/shard_map/all_gather | solution.py:36
  17.2 2.0 copy-start.3
  17.2 221.7 %reduce-scatter.3.cloned.1.call-start = ((), (), s32[]{:S(2)}) async-start(), calls=%async_computation.3 | async-start | bytes 4718592 | tf_op jit(solution)/shard_map/reduce_scatter | solution.py:41
  20.5 54.2 %copy-start.2 = (s32[16,16]{1,0:T(8,128)S(1)}, s32[16,16]{1,0:T(8,128)}, u32[]{:S(2)}) copy-start(s32[16,16]{1,0:T(8,128)} %param.9) | copy-start | bytes 3076
  22.3 3.2 %copy-start = (f32[1024,2048]{0,1:T(8,128)}, f32[1024,2048]{0,1:T(8,128)S(1)}, u32[]{:S(2)}) copy-start(f32[1024,2048]{0,1:T(8,128)S(1)} %get-tuple-element.5) | copy-start | bytes 25165828
  25.5 47.6 %collective-permute-start = (f32[1024,512]{0,1:T(8,128)}, f32[1024,512]{0,1:T(8,128)S(1)}, u32[]{:S(2)}, u32[]{:S(2)}) collective-permute-start(f32[1024,512]{0,1:T(8,128)} %get-tuple-element.6), channel_id=1, source_target_pairs={{0,1},{1,2},{2,3},{3,0},{4,5},{5,6},{6,7},{7,4},{8,9},{9,10},{10,1... | collective-permute-start | bytes 6291464 | tf_op jit(solution)/shard_map/ppermute | solution.py:16
  27.1 57.2 %collective-permute-start.1 = (f32[1024,512]{0,1:T(8,128)}, f32[1024,512]{0,1:T(8,128)}, u32[]{:S(2)}, u32[]{:S(2)}) collective-permute-start(f32[1024,512]{0,1:T(8,128)} %get-tuple-element.6), channel_id=1, source_target_pairs={{0,3},{1,0},{2,1},{3,2},{4,7},{5,4},{6,5},{7,6},{8,11},{9,8},{10,9... | collective-permute-start | bytes 6291464 | tf_op jit(solution)/shard_map/ppermute | solution.py:19
  73.1 46.6 %collective-permute-start.2 = (f32[1024,512]{0,1:T(8,128)S(1)}, f32[1024,512]{0,1:T(8,128)}, u32[]{:S(2)}, u32[]{:S(2)}) collective-permute-start(f32[1024,512]{0,1:T(8,128)S(1)} %collective-permute-done), channel_id=1, source_target_pairs={{0,1},{1,2},{2,3},{3,0},{4,5},{5,6},{6,7},{7,4},{8,9},{9,10},{10,1... | collective-permute-start | bytes 6291464 | tf_op jit(solution)/shard_map/ppermute | solution.py:16
  180.4 83.9 %reduce-scatter.5.cloned.1.call-start = ((), (), s32[]{:S(2)}) async-start(), calls=%async_computation.4 | async-start | bytes 655360 | tf_op jit(solution)/shard_map/reduce_scatter | solution.py:42
Sparse Core Ops, SparseCore 0:
  17.4 28.0 all-gather.1
  180.5 58.4 reduce-scatter.2
  241.5 22.7 reduce-scatter.4
